TPU v7x, 512 devices: a whole 4x4x16 slice. The times are simulated.
512 devices in a mesh: line: 32 (over z, core), scan: 16 (over x, y).
Axes of the slice: x: 4, y: 4, z: 16, core: 2. Of those that a mesh axis runs over, the one named last changes fastest.
Arguments:
- query_row: bfloat16 [32, 2048, 512], P('line', 'scan'), may hold values from -6 to 6
- key_row: bfloat16 [32, 2048, 512], P('line', 'scan'), may hold values from -6 to 6
- value_row: bfloat16 [32, 2048, 512], P('line', 'scan'), may hold values from -6 to 6
- decay_row: float32 [32, 2048, 4], P('line', 'scan'), may hold values from -2 to 0
- beta_row: float32 [32, 2048, 4], P('line', 'scan'), may hold values from 0.02 to 0.2
- gain_row: float32 [128], replicated, may hold values from 0.1 to 1.9
- query_col: bfloat16 [32, 16, 128, 512], P(None, 'scan', 'line'), may hold values from -6 to 6
- key_col: bfloat16 [32, 16, 128, 512], P(None, 'scan', 'line'), may hold values from -6 to 6
- decay_col: float32 [32, 16, 128, 4], P(None, 'scan', 'line'), may hold values from -2 to 0
- beta_col: float32 [32, 16, 128, 4], P(None, 'scan', 'line'), may hold values from 0.02 to 0.2
- gain_col: float32 [128], replicated, may hold values from 0.1 to 1.9
Outputs:
- mixed: bfloat16 [32, 2048, 512], P('line', 'scan')
All inputs are finite; a program needn't handle non-finite values.
Results may differ from a plain program's by a relative error of at most 0.0049.
Values may be sent and summed in bfloat16 or wider, within the bound.
No kernel may reach another device: no remote copies, remote signals or barrier semaphores. Data moves between devices by JAX's collectives and lax.ppermute only.
A program may use at most 64 MiB of HBM per device.

v0:
```python
import jax
import jax.numpy as jnp
from jax import lax
from jax.sharding import PartitionSpec as P

HIGHEST = lax.Precision.HIGHEST
BASE_BLOCK = 16


def from_behind(block, axis, distance):
    devices = range(lax.axis_size(axis))
    route = [(i - distance, i) for i in devices if i - distance in devices]
    return lax.ppermute(block, axis, route)


def matmul(spec, left, right):
    return jnp.einsum(spec, left, right, precision=HIGHEST)


def unit_lower_inverse(system):
    batch = system.shape[:-2]
    size = system.shape[-1]
    base = min(BASE_BLOCK, size)
    count = size // base
    assert count * base == size and count & count - 1 == 0
    eye = jnp.eye(base, dtype=jnp.float32)
    grid = system.reshape(batch + (count, base, count, base))
    diagonal = jnp.moveaxis(jnp.diagonal(grid, axis1=-4, axis2=-2), -1, -3)
    lower = diagonal - eye
    inverse = eye - lower
    power = lower
    reach = 2
    while reach < base:
        power = matmul("...ij,...jk->...ik", power, power)
        inverse = inverse + matmul("...ij,...jk->...ik", inverse, power)
        reach *= 2
    width = base
    while width < size:
        pairs = size // (2 * width)
        grid = system.reshape(batch + (pairs, 2, width, pairs, 2, width))
        coupling = jnp.moveaxis(jnp.diagonal(grid, axis1=-6, axis2=-3), -1, -5)[..., 1, :, 0, :]
        halves = inverse.reshape(batch + (pairs, 2, width, width))
        upper_inverse = halves[..., 0, :, :]
        lower_inverse = halves[..., 1, :, :]
        mixed = -matmul(
            "...ij,...jk->...ik",
            matmul("...ij,...jk->...ik", lower_inverse, coupling),
            upper_inverse,
        )
        top = jnp.concatenate([upper_inverse, jnp.zeros_like(upper_inverse)], axis=-1)
        bottom = jnp.concatenate([mixed, lower_inverse], axis=-1)
        inverse = jnp.concatenate([top, bottom], axis=-2)
        width *= 2
    return inverse.reshape(batch + (size, size))


def block_system(key_block, log_decay, beta_block):
    key_unit = key_block / jnp.sqrt(jnp.sum(key_block * key_block, axis=-1, keepdims=True) + 1e-06)
    cumulative = jnp.cumsum(log_decay, axis=-1)
    sequence_length = key_block.shape[1]
    lower_mask = jnp.tril(jnp.ones((sequence_length, sequence_length), dtype=jnp.bool_))
    strict = jnp.tril(jnp.ones((sequence_length, sequence_length), dtype=jnp.bool_), -1)
    spread = cumulative[:, :, None] - cumulative[:, None, :]
    ratios = jnp.where(lower_mask, jnp.exp(jnp.where(lower_mask, spread, 0.0)), 0.0)
    key_inner = matmul("bik,bjk->bij", key_unit, key_unit)
    system = jnp.where(strict, beta_block[:, :, None] * ratios * key_inner, 0.0) + jnp.eye(
        sequence_length, dtype=jnp.float32
    )
    return (key_unit, cumulative, ratios, unit_lower_inverse(system))


def block_terms(query_block, key_block, value_block, log_decay, beta_block):
    key_unit, cumulative, ratios, system_inverse = block_system(key_block, log_decay, beta_block)
    growth = jnp.exp(cumulative)
    right_side = jnp.concatenate(
        [beta_block[:, :, None] * value_block, (beta_block * growth)[:, :, None] * key_unit],
        axis=-1,
    )
    solved = matmul("bij,bjv->biv", system_inverse, right_side)
    value_size = value_block.shape[-1]
    updates = solved[:, :, :value_size]
    weighted = solved[:, :, value_size:]
    attend = ratios * matmul("bik,bjk->bij", query_block, key_unit)
    local_out = matmul("bij,bjv->biv", attend, updates)
    state_query = growth[:, :, None] * query_block - matmul("bij,bjk->bik", attend, weighted)
    key_tail = jnp.exp(cumulative[:, -1:] - cumulative)[:, :, None] * key_unit
    return (local_out, state_query, key_tail, weighted, updates, growth[:, -1])


def column_operator(query_block, key_block, log_decay, beta_block):
    key_unit, cumulative, ratios, system_inverse = block_system(key_block, log_decay, beta_block)
    attend = ratios * matmul("bik,bjk->bij", query_block, key_unit)
    return matmul("bij,bjk->bik", attend, system_inverse) * beta_block[:, None, :]


def to_heads(array, leading_count, sequence_length, head_count, head_size):
    shaped = array.astype(jnp.float32).reshape(
        leading_count, sequence_length, head_count, head_size
    )
    return shaped.transpose(0, 2, 1, 3).reshape(
        leading_count * head_count, sequence_length, head_size
    )


def gates_to_heads(array, leading_count, sequence_length, head_count):
    return array.transpose(0, 2, 1).reshape(leading_count * head_count, sequence_length)


def from_heads(array, leading_count, sequence_length, head_count, head_size):
    return array.reshape(leading_count, head_count, sequence_length, head_size).transpose(
        0, 2, 1, 3
    )


def head_norm(array, gain):
    return array * lax.rsqrt(jnp.mean(array * array, axis=-1, keepdims=True) + 1e-05) * gain


def prefix_states(transfer, offset):
    scan_count = lax.axis_size("scan")
    head_size = offset.shape[-1]
    distance = 1
    while distance < scan_count:
        if 2 * distance < scan_count:
            arrived = from_behind(jnp.concatenate([transfer, offset], axis=-1), "scan", distance)
            composed = matmul("bij,bjv->biv", transfer, arrived)
            transfer = composed[:, :, :head_size]
            offset = composed[:, :, head_size:] + offset
        else:
            arrived = from_behind(offset, "scan", distance)
            offset = matmul("bij,bjv->biv", transfer, arrived) + offset
        distance *= 2
    return from_behind(offset, "scan", 1)


def shards(
    query_row,
    key_row,
    value_row,
    decay_row,
    beta_row,
    gain_row,
    query_col,
    key_col,
    decay_col,
    beta_col,
    gain_col,
):
    row_count, segment, features = query_row.shape
    head_size = gain_row.shape[0]
    head_count = features // head_size
    line_count = lax.axis_size("line")
    total_rows = query_col.shape[0]
    column_count = query_col.shape[2]

    def columns(array):
        return array.reshape(total_rows, column_count, -1).transpose(1, 0, 2)

    local_out, state_query, key_tail, weighted, updates, ending = block_terms(
        to_heads(query_row, row_count, segment, head_count, head_size),
        to_heads(key_row, row_count, segment, head_count, head_size),
        to_heads(value_row, row_count, segment, head_count, head_size),
        gates_to_heads(decay_row, row_count, segment, head_count),
        gates_to_heads(beta_row, row_count, segment, head_count),
    )
    identity = jnp.broadcast_to(
        jnp.eye(head_size, dtype=jnp.float32), (row_count * head_count, head_size, head_size)
    )
    transfer = ending[:, None, None] * identity - matmul("bjk,bjl->bkl", key_tail, weighted)
    offset = matmul("bjk,bjv->bkv", key_tail, updates)
    operator = column_operator(
        to_heads(columns(query_col), column_count, total_rows, head_count, head_size),
        to_heads(columns(key_col), column_count, total_rows, head_count, head_size),
        gates_to_heads(columns(decay_col), column_count, total_rows, head_count),
        gates_to_heads(columns(beta_col), column_count, total_rows, head_count),
    )
    incoming = prefix_states(transfer, offset)
    row_out = local_out + matmul("bik,bkv->biv", state_query, incoming)
    row_scan = from_heads(row_out, row_count, segment, head_count, head_size)
    values_col = (
        head_norm(row_scan, gain_row).reshape(row_count, segment, features).astype(jnp.bfloat16)
    )
    arranged = values_col.reshape(row_count, line_count, segment // line_count, features)
    column_values = lax.all_to_all(arranged, "line", split_axis=1, concat_axis=0, tiled=True)
    col_out = matmul(
        "bij,bjv->biv",
        operator,
        to_heads(columns(column_values), column_count, total_rows, head_count, head_size),
    )
    col_scan = from_heads(col_out, column_count, total_rows, head_count, head_size)
    normed = (
        head_norm(col_scan, gain_col)
        .transpose(1, 0, 2, 3)
        .reshape(total_rows, 1, column_count, features)
        .astype(jnp.bfloat16)
    )
    returned = lax.all_to_all(normed, "line", split_axis=0, concat_axis=1, tiled=True)
    return returned.reshape(row_count, segment, features)


def solution(mesh):
    placed = (
        P("line", "scan", None),
        P("line", "scan", None),
        P("line", "scan", None),
        P("line", "scan", None),
        P("line", "scan", None),
        P(),
        P(None, "scan", "line", None),
        P(None, "scan", "line", None),
        P(None, "scan", "line", None),
        P(None, "scan", "line", None),
        P(),
    )
    return jax.shard_map(
        shards, mesh=mesh, in_specs=placed, out_specs=P("line", "scan", None), check_vma=False
    )
```

profile of v0, /device:TPU:6, one launch (start us, length us, event | category | flops | bytes accessed | tf_op | source)
XLA Modules:
  0.0 160.5 jit_solution(16315347786779798503)
XLA Ops:
  0.0 0.8 fusion.86
  1.2 1.0 reduce_window_sum.23
  2.1 1.5 fusion.5
  4.2 1.7 %copy.195 = f32[4,8,16,8,16]{4,2,3,1,0:T(8,128)} copy(f32[4,8,16,8,16]{4,3,2,1,0:T(8,128)S(1)} %reshape.334) | data formatting | bytes 524288 | tf_op jit(solution)/shard_map/reshape | solution.py:27
  5.9 2.2 %gather_fusion.1 = f32[8,4,16,16]{3,2,1,0:T(8,128)S(1)} fusion(f32[4,16,16,8,8]{2,1,4,3,0:T(8,128)} %bitcast.193, s32[8]{0:T(128)S(1)} %or_bitcast_fusion.1), kind=kCustom, calls=%fused_computation.1 | custom fusion | bytes 65600 | tf_op jit(solution)/shard_map/jit(diagonal)/gather | solution.py:28
  9.3 2.7 %reshape.336 = f32[4,4,2,16,4,2,16]{6,5,4,3,2,1,0:T(2,128)S(1)} reshape(f32[4,128,128]{2,1,0:T(8,128)S(1)} %fusion.5) | data formatting | bytes 524288 | tf_op jit(solution)/shard_map/reshape | solution.py:40
  12.0 1.8 %reshape.338 = f32[4,2,2,32,2,2,32]{6,5,4,3,2,1,0:T(2,128)} reshape(f32[4,128,128]{2,1,0:T(8,128)S(1)} %fusion.5) | data formatting | bytes 524288 | tf_op jit(solution)/shard_map/reshape | solution.py:40
  13.8 1.1 transpose.144
  16.3 1.7 %copy.194 = f32[4,4,2,16,4,2,16]{6,3,4,1,5,2,0:T(8,128)} copy(f32[4,4,2,16,4,2,16]{6,5,4,3,2,1,0:T(2,128)S(1)} %reshape.336) | data formatting | bytes 524288 | tf_op jit(solution)/shard_map/reshape | solution.py:40
  18.0 2.2 %gather_fusion.2 = f32[4,4,2,16,2,16]{5,3,4,2,1,0:T(8,128)S(1)} fusion(f32[4,2,16,2,16,4,4]{4,2,6,5,3,1,0:T(8,128)} %bitcast.192, s32[4]{0:T(128)S(1)} %or_bitcast_fusion), kind=kCustom, calls=%fused_computation.2 | custom fusion | bytes 131104 | tf_op jit(solution)/shard_map/jit(diagonal)/gather | solution.py:41
  22.9 1.0 slice.234
  25.7 0.8 fusion.32
  26.8 0.7 convolution_subtract_fusion
  27.5 0.8 pad_maximum_fusion
  28.4 3.7 %collective-permute-start = (f32[4,128,256]{2,1,0:T(8,128)}, f32[4,128,256]{2,1,0:T(8,128)}, u32[]{:S(2)}, u32[]{:S(2)}) collective-permute-start(f32[4,128,256]{2,1,0:T(8,128)} %pad_maximum_fusion), channel_id=1, source_target_pairs={{0,1},{1,2},{2,3},{3,4},{4,5},{5,6},{6,7},{7,8},{8,9},{9,10},{10,1... | collective-permute-start | bytes 1572872 | tf_op jit(solution)/shard_map/ppermute | solution.py:13
  37.7 8.6 %collective-permute-done = f32[4,128,256]{2,1,0:T(8,128)} collective-permute-done((f32[4,128,256]{2,1,0:T(8,128)}, f32[4,128,256]{2,1,0:T(8,128)}, u32[]{:S(2)}, u32[]{:S(2)}) %collective-permute-start) | collective-permute-done | bytes 524320 | tf_op jit(solution)/shard_map/ppermute | solution.py:13
  46.3 2.1 %fusion.93 = f32[4,128,256]{1,2,0:T(8,128)S(1)} fusion(f32[4,128,128]{2,1,0:T(8,128)S(1)} %convolution_subtract_fusion, f32[4,128,256]{2,1,0:T(8,128)} %collective-permute-done), kind=kOutput, calls=%fused_computation.184 | convolution fusion | flops 201326592 | bytes 1310720 | tf_op jit(solution)/shard_map/bij,bjv->biv/dot_general | solution.py:17
  48.5 3.0 %collective-permute-start.1 = (f32[4,128,256]{1,2,0:T(8,128)S(1)}, f32[4,128,256]{1,2,0:T(8,128)S(1)}, u32[]{:S(2)}, u32[]{:S(2)}) collective-permute-start(f32[4,128,256]{1,2,0:T(8,128)S(1)} %pad_maximum_fusion.1), channel_id=1, source_target_pairs={{0,2},{1,3},{2,4},{3,5},{4,6},{5,7},{6,8},{7,9},{8,10},{9,11},{10,... | collective-permute-start | bytes 1572872 | tf_op jit(solution)/shard_map/ppermute | solution.py:13
  52.6 13.0 %collective-permute-done.1 = f32[4,128,256]{1,2,0:T(8,128)S(1)} collective-permute-done((f32[4,128,256]{1,2,0:T(8,128)S(1)}, f32[4,128,256]{1,2,0:T(8,128)S(1)}, u32[]{:S(2)}, u32[]{:S(2)}) %collective-permute-start.1) | collective-permute-done | bytes 524320 | tf_op jit(solution)/shard_map/ppermute | solution.py:13
  66.3 0.8 pad_maximum_fusion.2
  67.1 1.3 collective-permute-start.2
  69.6 11.5 %collective-permute-done.2 = f32[4,128,256]{1,2,0:T(8,128)} collective-permute-done((f32[4,128,256]{1,2,0:T(8,128)}, f32[4,128,256]{1,2,0:T(8,128)}, u32[]{:S(2)}, u32[]{:S(2)}) %collective-permute-start.2) | collective-permute-done | bytes 524320 | tf_op jit(solution)/shard_map/ppermute | solution.py:13
  81.2 1.7 %fusion.75 = f32[4,128,256]{2,1,0:T(8,128)S(1)} fusion(f32[4,128,256]{1,2,0:T(8,128)} %collective-permute-done.2, f32[4,128,256]{1,2,0:T(8,128)S(1)} %fusion.77), kind=kOutput, calls=%fused_computation.166 | convolution fusion | flops 201326592 | bytes 1310720 | tf_op jit(solution)/shard_map/bij,bjv->biv/dot_general | solution.py:17
  83.0 1.3 collective-permute-start.3
  85.2 7.6 %collective-permute-done.3 = f32[4,128,128]{1,2,0:T(8,128)S(1)} collective-permute-done((f32[4,128,128]{1,2,0:T(8,128)S(1)}, f32[4,128,128]{1,2,0:T(8,128)S(1)}, u32[]{:S(2)}, u32[]{:S(2)}) %collective-permute-start.3) | collective-permute-done | bytes 262176 | tf_op jit(solution)/shard_map/ppermute | solution.py:13
  93.6 2.1 %collective-permute-start.4 = (f32[4,128,128]{1,2,0:T(8,128)S(1)}, f32[4,128,128]{1,2,0:T(8,128)S(1)}, u32[]{:S(2)}, u32[]{:S(2)}) collective-permute-start(f32[4,128,128]{1,2,0:T(8,128)S(1)} %convolution_add_fusion.7), channel_id=1, source_target_pairs={{0,1},{1,2},{2,3},{3,4},{4,5},{5,6},{6,7},{7,8},{8,9},{9,10},{10,1... | collective-permute-start | bytes 786440 | tf_op jit(solution)/shard_map/ppermute | solution.py:13
  96.1 8.0 %collective-permute-done.4 = f32[4,128,128]{1,2,0:T(8,128)S(1)} collective-permute-done((f32[4,128,128]{1,2,0:T(8,128)S(1)}, f32[4,128,128]{1,2,0:T(8,128)S(1)}, u32[]{:S(2)}, u32[]{:S(2)}) %collective-permute-start.4) | collective-permute-done | bytes 262176 | tf_op jit(solution)/shard_map/ppermute | solution.py:13
  105.0 0.7 convert_element_type.90
  105.7 15.5 %all-to-all-start = ((bf16[1,32,4,512]{3,2,0,1:T(4,128)(2,1)}), bf16[1,32,4,512]{3,2,0,1:T(4,128)(2,1)S(1)}, u32[]{:S(2)}, u32[]{:S(2)}) async-start(bf16[1,32,4,512]{3,2,0,1:T(4,128)(2,1)} %bitcast.66), calls=%async_computation | async-start | bytes 262144 | tf_op jit(solution)/shard_map/all_to_all | solution.py:184
  122.2 16.2 %all-to-all-done = bf16[1,32,4,512]{3,2,0,1:T(4,128)(2,1)S(1)} async-done(((bf16[1,32,4,512]{3,2,0,1:T(4,128)(2,1)}), bf16[1,32,4,512]{3,2,0,1:T(4,128)(2,1)S(1)}, u32[]{:S(2)}, u32[]{:S(2)}) %all-to-all-start) | async-done | bytes 131104 | tf_op jit(solution)/shard_map/all_to_all | solution.py:184
  139.6 20.2 %all_to_all.8 = bf16[32,1,4,512]{3,2,1,0:T(4,128)(2,1)S(1)} all-to-all(bf16[32,1,4,512]{3,2,1,0:T(4,128)(2,1)S(1)} %copy.160), channel_id=1, replica_groups=mesh['line'=32,'scan'=16] {'line'}, dimensions={0} | all-to-all | bytes 262144 | tf_op jit(solution)/shard_map/all_to_all | solution.py:197
  159.8 0.7 reshape.350
  (163 shorter events, 21.4 us)
Async XLA Ops:
  1.0 25.8 %copy-start.20 = (f32[4,128]{1,0:T(4,128)}, f32[4,128]{1,0:T(4,128)S(1)}, u32[]{:S(2)}) copy-start(f32[4,128]{1,0:T(4,128)S(1)} %sqrt_bitcast_fusion) | copy-start | bytes 6148
  1.1 4.8 %copy-start.17 = (pred[128,128]{1,0:T(8,128)(4,1)}, pred[128,128]{1,0:T(8,128)(4,1)S(1)}, u32[]{:S(2)}) copy-start(pred[128,128]{1,0:T(8,128)(4,1)S(1)} %get-tuple-element.57) | copy-start | bytes 49156
  22.2 2.4 %copy-start.2 = (bf16[1,128,512]{2,1,0:T(8,128)(2,1)S(1)}, bf16[1,128,512]{2,1,0:T(8,128)(2,1)}, u32[]{:S(2)}) copy-start(bf16[1,128,512]{2,1,0:T(8,128)(2,1)} %param.13) | copy-start | bytes 393220
  22.3 2.3 %copy-start.22 = (f32[1,128,4]{1,2,0:T(4,128)S(1)}, f32[1,128,4]{1,2,0:T(4,128)}, u32[]{:S(2)}) copy-start(f32[1,128,4]{1,2,0:T(4,128)} %param.15) | copy-start | bytes 6148
  25.6 6.4 %copy-start.1 = (bf16[1,128,512]{2,1,0:T(8,128)(2,1)S(1)}, bf16[1,128,512]{2,1,0:T(8,128)(2,1)}, u32[]{:S(2)}) copy-start(bf16[1,128,512]{2,1,0:T(8,128)(2,1)} %param.11) | copy-start | bytes 393220
  25.7 7.1 %copy-start.7 = (bf16[32,1,4,512]{3,2,1,0:T(4,128)(2,1)S(1)}, bf16[32,1,4,512]{3,2,1,0:T(4,128)(2,1)}, u32[]{:S(2)}) copy-start(bf16[32,1,4,512]{3,2,1,0:T(4,128)(2,1)} %param.18) | copy-start | bytes 393220
  26.6 6.5 %copy-start.25 = (f32[32,1,4,4]{0,3,2,1:T(4,128)S(1)}, f32[32,1,4,4]{0,3,2,1:T(4,128)}, u32[]{:S(2)}) copy-start(f32[32,1,4,4]{0,3,2,1:T(4,128)} %param.19) | copy-start | bytes 6148
  26.6 6.7 %copy-start.19 = (f32[32,1,4,4]{0,3,2,1:T(4,128)S(1)}, f32[32,1,4,4]{0,3,2,1:T(4,128)}, u32[]{:S(2)}) copy-start(f32[32,1,4,4]{0,3,2,1:T(4,128)} %param.20) | copy-start | bytes 6148
  28.4 18.0 %collective-permute-start = (f32[4,128,256]{2,1,0:T(8,128)}, f32[4,128,256]{2,1,0:T(8,128)}, u32[]{:S(2)}, u32[]{:S(2)}) collective-permute-start(f32[4,128,256]{2,1,0:T(8,128)} %pad_maximum_fusion), channel_id=1, source_target_pairs={{0,1},{1,2},{2,3},{3,4},{4,5},{5,6},{6,7},{7,8},{8,9},{9,10},{10,1... | collective-permute-start | bytes 1572872 | tf_op jit(solution)/shard_map/ppermute | solution.py:13
  48.5 17.1 %collective-permute-start.1 = (f32[4,128,256]{1,2,0:T(8,128)S(1)}, f32[4,128,256]{1,2,0:T(8,128)S(1)}, u32[]{:S(2)}, u32[]{:S(2)}) collective-permute-start(f32[4,128,256]{1,2,0:T(8,128)S(1)} %pad_maximum_fusion.1), channel_id=1, source_target_pairs={{0,2},{1,3},{2,4},{3,5},{4,6},{5,7},{6,8},{7,9},{8,10},{9,11},{10,... | collective-permute-start | bytes 1572872 | tf_op jit(solution)/shard_map/ppermute | solution.py:13
  52.6 15.8 %copy-start.13 = (bf16[1,128,128]{2,1,0:T(8,128)(2,1)S(1)}, bf16[1,128,128]{2,1,0:T(8,128)(2,1)}, u32[]{:S(2)}) copy-start(bf16[1,128,128]{2,1,0:T(8,128)(2,1)} %get-tuple-element.41) | copy-start | bytes 98308
  52.6 15.8 %copy-start.14 = (bf16[1,128,128]{2,1,0:T(8,128)(2,1)S(1)}, bf16[1,128,128]{2,1,0:T(8,128)(2,1)}, u32[]{:S(2)}) copy-start(bf16[1,128,128]{2,1,0:T(8,128)(2,1)} %get-tuple-element.42) | copy-start | bytes 98308
  52.6 15.8 %copy-start.15 = (bf16[1,128,128]{2,1,0:T(8,128)(2,1)S(1)}, bf16[1,128,128]{2,1,0:T(8,128)(2,1)}, u32[]{:S(2)}) copy-start(bf16[1,128,128]{2,1,0:T(8,128)(2,1)} %get-tuple-element.43) | copy-start | bytes 98308
  52.6 15.8 %copy-start.16 = (bf16[1,128,128]{2,1,0:T(8,128)(2,1)S(1)}, bf16[1,128,128]{2,1,0:T(8,128)(2,1)}, u32[]{:S(2)}) copy-start(bf16[1,128,128]{2,1,0:T(8,128)(2,1)} %get-tuple-element.44) | copy-start | bytes 98308
  66.2 2.9 %copy-start.18 = (pred[128,128]{1,0:T(8,128)(4,1)S(1)}, pred[128,128]{1,0:T(8,128)(4,1)}, u32[]{:S(2)}) copy-start(pred[128,128]{1,0:T(8,128)(4,1)} %copy-done.17) | copy-start | bytes 49156
  66.2 2.9 %copy-start.21 = (f32[4,128]{1,0:T(4,128)S(1)}, f32[4,128]{1,0:T(4,128)}, u32[]{:S(2)}) copy-start(f32[4,128]{1,0:T(4,128)} %copy-done.20) | copy-start | bytes 6148
  67.1 14.1 %collective-permute-start.2 = (f32[4,128,256]{1,2,0:T(8,128)}, f32[4,128,256]{1,2,0:T(8,128)}, u32[]{:S(2)}, u32[]{:S(2)}) collective-permute-start(f32[4,128,256]{1,2,0:T(8,128)} %pad_maximum_fusion.2), channel_id=1, source_target_pairs={{0,4},{1,5},{2,6},{3,7},{4,8},{5,9},{6,10},{7,11},{8,12},{9,13},{1... | collective-permute-start | bytes 1572872 | tf_op jit(solution)/shard_map/ppermute | solution.py:13
  82.8 12.8 %copy-start.5 = (f32[1,128,128]{2,1,0:T(8,128)S(1)}, f32[1,128,128]{2,1,0:T(8,128)}, u32[]{:S(2)}) copy-start(f32[1,128,128]{2,1,0:T(8,128)} %get-tuple-element.31) | copy-start | bytes 196612
  82.8 12.8 %copy-start.6 = (f32[1,128,128]{2,1,0:T(8,128)S(1)}, f32[1,128,128]{2,1,0:T(8,128)}, u32[]{:S(2)}) copy-start(f32[1,128,128]{2,1,0:T(8,128)} %get-tuple-element.32) | copy-start | bytes 196612
  83.0 9.8 %collective-permute-start.3 = (f32[4,128,128]{1,2,0:T(8,128)S(1)}, f32[4,128,128]{1,2,0:T(8,128)S(1)}, u32[]{:S(2)}, u32[]{:S(2)}) collective-permute-start(f32[4,128,128]{1,2,0:T(8,128)S(1)} %add.162), channel_id=1, source_target_pairs={{0,8},{1,9},{2,10},{3,11},{4,12},{5,13},{6,14},{7,15},{16,24},{17,... | collective-permute-start | bytes 786440 | tf_op jit(solution)/shard_map/ppermute | solution.py:13
  84.6 20.2 %copy-start.30 = (f32[128]{0:T(128)S(1)}, f32[128]{0:T(128)}, u32[]{:S(2)}) copy-start(f32[128]{0:T(128)} %param.16) | copy-start | bytes 1540
  93.5 27.8 %copy-start.9 = (bf16[4,32,128]{2,1,0:T(8,128)(2,1)S(1)}, bf16[4,32,128]{2,1,0:T(8,128)(2,1)}, u32[]{:S(2)}) copy-start(bf16[4,32,128]{2,1,0:T(8,128)(2,1)} %get-tuple-element.45) | copy-start | bytes 98308
  93.5 27.8 %copy-start.10 = (bf16[4,32,128]{2,1,0:T(8,128)(2,1)S(1)}, bf16[4,32,128]{2,1,0:T(8,128)(2,1)}, u32[]{:S(2)}) copy-start(bf16[4,32,128]{2,1,0:T(8,128)(2,1)} %get-tuple-element.46) | copy-start | bytes 98308
  93.5 27.8 %copy-start.11 = (bf16[4,32,128]{2,1,0:T(8,128)(2,1)S(1)}, bf16[4,32,128]{2,1,0:T(8,128)(2,1)}, u32[]{:S(2)}) copy-start(bf16[4,32,128]{2,1,0:T(8,128)(2,1)} %get-tuple-element.47) | copy-start | bytes 98308
  93.5 27.8 %copy-start.12 = (bf16[4,32,128]{2,1,0:T(8,128)(2,1)S(1)}, bf16[4,32,128]{2,1,0:T(8,128)(2,1)}, u32[]{:S(2)}) copy-start(bf16[4,32,128]{2,1,0:T(8,128)(2,1)} %get-tuple-element.48) | copy-start | bytes 98308
  93.5 27.8 %copy-start.4 = (f32[4,128,128]{2,1,0:T(8,128)S(1)}, f32[4,128,128]{2,1,0:T(8,128)}, u32[]{:S(2)}) copy-start(f32[4,128,128]{2,1,0:T(8,128)} %copy-done.3) | copy-start | bytes 786436
  93.5 27.8 %copy-start.24 = (f32[16,32]{1,0:T(8,128)S(1)}, f32[16,32]{1,0:T(8,128)}, u32[]{:S(2)}) copy-start(f32[16,32]{1,0:T(8,128)} %copy-done.23) | copy-start | bytes 6148
  93.5 27.8 %copy-start.27 = (f32[16,32]{1,0:T(8,128)S(1)}, f32[16,32]{1,0:T(8,128)}, u32[]{:S(2)}) copy-start(f32[16,32]{1,0:T(8,128)} %copy-done.26) | copy-start | bytes 6148
  93.6 27.8 %copy-start.29 = (pred[32,32]{1,0:T(8,128)(4,1)S(1)}, pred[32,32]{1,0:T(8,128)(4,1)}, u32[]{:S(2)}) copy-start(pred[32,32]{1,0:T(8,128)(4,1)} %copy-done.28) | copy-start | bytes 3076
  93.6 10.5 %collective-permute-start.4 = (f32[4,128,128]{1,2,0:T(8,128)S(1)}, f32[4,128,128]{1,2,0:T(8,128)S(1)}, u32[]{:S(2)}, u32[]{:S(2)}) collective-permute-start(f32[4,128,128]{1,2,0:T(8,128)S(1)} %convolution_add_fusion.7), channel_id=1, source_target_pairs={{0,1},{1,2},{2,3},{3,4},{4,5},{5,6},{6,7},{7,8},{8,9},{9,10},{10,1... | collective-permute-start | bytes 786440 | tf_op jit(solution)/shard_map/ppermute | solution.py:13
  105.7 32.8 %all-to-all-start = ((bf16[1,32,4,512]{3,2,0,1:T(4,128)(2,1)}), bf16[1,32,4,512]{3,2,0,1:T(4,128)(2,1)S(1)}, u32[]{:S(2)}, u32[]{:S(2)}) async-start(bf16[1,32,4,512]{3,2,0,1:T(4,128)(2,1)} %bitcast.66), calls=%async_computation | async-start | bytes 262144 | tf_op jit(solution)/shard_map/all_to_all | solution.py:184
  121.4 17.8 %copy-start.31 = (f32[128]{0:T(128)S(1)}, f32[128]{0:T(128)}, u32[]{:S(2)}) copy-start(f32[128]{0:T(128)} %param.21) | copy-start | bytes 1540
  (6 other events, 9.3 us)
where the time goes:
time: 161 us; the launch traced here: 160 us
  waiting for transfers between devices  65 us (40%)
  starting transfers between devices  26.8 us (17%)
  local copies, waits for them, and re-layouts  23.5 us (15%)
  blocking collectives  20.2 us (13%)
  matrix products  19.1 us (12%)
  other arithmetic  4.77 us (3%)
    ppermute x5, waiting for transfers between devices, from_behind(): return lax.ppermute(block, axis, route)  48.8 us
    all_to_all x1, blocking collectives, shards(): lax.all_to_all(normed, 'line', split_axis=0, concat_axis=1, tiled=True)  20.2 us
    dot_general x36, matrix products, matmul(): return jnp.einsum(spec, left, right, precision=HIGHEST)  19.1 us
    all_to_all x1, waiting for transfers between devices, shards(): lax.all_to_all(arranged, 'line', split_axis=1, concat_axis=0, tiled=True)  16.2 us
    all_to_all x1, starting transfers between devices, shards(): lax.all_to_all(arranged, 'line', split_axis=1, concat_axis=0, tiled=True)  15.5 us
    ppermute x5, starting transfers between devices, from_behind(): return lax.ppermute(block, axis, route)  11.3 us
    reshape x4, local copies, waits for them, and re-layouts, unit_lower_inverse(): grid = system.reshape(batch + (pairs, 2, width, pairs, 2, width))  6.38 us
  transfers between devices with their start and end apart: 6, of which 6 were waited for; matrix products, arithmetic and copies ran while one was open for 6% of the time, Pallas kernels for 0%

commit v1 on v0

--- a/solution.py
+++ b/solution.py
@@ -194,7 +194,9 @@
         .reshape(total_rows, 1, column_count, features)
         .astype(jnp.bfloat16)
     )
-    returned = lax.all_to_all(normed, "line", split_axis=0, concat_axis=1, tiled=True)
+    cells = jnp.split(normed, lax.axis_size("line"), axis=0)
+    arrived_2 = lax.all_to_all(jnp.stack(cells), "line", 0, 0)
+    returned = jnp.concatenate(arrived_2, axis=1)
     return returned.reshape(row_count, segment, features)
 
 

time: 161 us -> 162 us (level)
    another operation x7 -> x41, local copies, waits for them, and re-layouts: 2.26 us -> 3.32 us
where the time goes in v1:
time: 162 us; the launch traced here: 161 us
  waiting for transfers between devices  64.8 us (40%)
  starting transfers between devices  27 us (17%)
  local copies, waits for them, and re-layouts  24.2 us (15%)
  blocking collectives  20.2 us (12%)
  matrix products  19.1 us (12%)
  other arithmetic  4.79 us (3%)
    ppermute x5, waiting for transfers between devices, from_behind(): return lax.ppermute(block, axis, route)  48.8 us
    all_to_all x1, blocking collectives, shards(): arrived_2 = lax.all_to_all(jnp.stack(cells), 'line', 0, 0)  20.2 us
    dot_general x36, matrix products, matmul(): return jnp.einsum(spec, left, right, precision=HIGHEST)  19.1 us
    all_to_all x1, waiting for transfers between devices, shards(): lax.all_to_all(arranged, 'line', split_axis=1, concat_axis=0, tiled=True)  16 us
    all_to_all x1, starting transfers between devices, shards(): lax.all_to_all(arranged, 'line', split_axis=1, concat_axis=0, tiled=True)  15.7 us
    ppermute x5, starting transfers between devices, from_behind(): return lax.ppermute(block, axis, route)  11.3 us
    reshape x4, local copies, waits for them, and re-layouts, unit_lower_inverse(): grid = system.reshape(batch + (pairs, 2, width, pairs, 2, width))  6.39 us
  transfers between devices with their start and end apart: 6, of which 6 were waited for; matrix products, arithmetic and copies ran while one was open for 6% of the time, Pallas kernels for 0%

profile of v1, /device:TPU:6, one launch (start us, length us, event | category | flops | bytes accessed | tf_op | source)
XLA Modules:
  0.0 161.3 jit_solution(4736426757627806194)
XLA Ops:
  0.0 0.8 fusion.88
  1.2 1.0 reduce_window_sum.23
  2.1 1.5 fusion.5
  4.2 1.7 %copy.192 = f32[4,8,16,8,16]{4,2,3,1,0:T(8,128)} copy(f32[4,8,16,8,16]{4,3,2,1,0:T(8,128)S(1)} %reshape.391) | data formatting | bytes 524288 | tf_op jit(solution)/shard_map/reshape | solution.py:27
  5.9 2.2 %gather_fusion.1 = f32[8,4,16,16]{3,2,1,0:T(8,128)S(1)} fusion(f32[4,16,16,8,8]{2,1,4,3,0:T(8,128)} %bitcast.191, s32[8]{0:T(128)S(1)} %or_bitcast_fusion.1), kind=kCustom, calls=%fused_computation.1 | custom fusion | bytes 65600 | tf_op jit(solution)/shard_map/jit(diagonal)/gather | solution.py:28
  9.3 2.7 %reshape.393 = f32[4,4,2,16,4,2,16]{6,5,4,3,2,1,0:T(2,128)S(1)} reshape(f32[4,128,128]{2,1,0:T(8,128)S(1)} %fusion.5) | data formatting | bytes 524288 | tf_op jit(solution)/shard_map/reshape | solution.py:40
  12.0 1.8 %reshape.395 = f32[4,2,2,32,2,2,32]{6,5,4,3,2,1,0:T(2,128)} reshape(f32[4,128,128]{2,1,0:T(8,128)S(1)} %fusion.5) | data formatting | bytes 524288 | tf_op jit(solution)/shard_map/reshape | solution.py:40
  13.8 1.1 transpose.144
  16.3 1.7 %copy.191 = f32[4,4,2,16,4,2,16]{6,3,4,1,5,2,0:T(8,128)} copy(f32[4,4,2,16,4,2,16]{6,5,4,3,2,1,0:T(2,128)S(1)} %reshape.393) | data formatting | bytes 524288 | tf_op jit(solution)/shard_map/reshape | solution.py:40
  18.0 2.2 %gather_fusion.2 = f32[4,4,2,16,2,16]{5,3,4,2,1,0:T(8,128)S(1)} fusion(f32[4,2,16,2,16,4,4]{4,2,6,5,3,1,0:T(8,128)} %bitcast.190, s32[4]{0:T(128)S(1)} %or_bitcast_fusion), kind=kCustom, calls=%fused_computation.2 | custom fusion | bytes 131104 | tf_op jit(solution)/shard_map/jit(diagonal)/gather | solution.py:41
  22.9 1.0 slice.266
  25.7 0.8 fusion.32
  26.8 0.7 convolution_subtract_fusion
  27.6 0.8 pad_maximum_fusion
  28.4 3.7 %collective-permute-start = (f32[4,128,256]{2,1,0:T(8,128)}, f32[4,128,256]{2,1,0:T(8,128)}, u32[]{:S(2)}, u32[]{:S(2)}) collective-permute-start(f32[4,128,256]{2,1,0:T(8,128)} %pad_maximum_fusion), channel_id=1, source_target_pairs={{0,1},{1,2},{2,3},{3,4},{4,5},{5,6},{6,7},{7,8},{8,9},{9,10},{10,1... | collective-permute-start | bytes 1572872 | tf_op jit(solution)/shard_map/ppermute | solution.py:13
  37.7 8.7 %collective-permute-done = f32[4,128,256]{2,1,0:T(8,128)} collective-permute-done((f32[4,128,256]{2,1,0:T(8,128)}, f32[4,128,256]{2,1,0:T(8,128)}, u32[]{:S(2)}, u32[]{:S(2)}) %collective-permute-start) | collective-permute-done | bytes 524320 | tf_op jit(solution)/shard_map/ppermute | solution.py:13
  46.4 2.1 %fusion.95 = f32[4,128,256]{1,2,0:T(8,128)S(1)} fusion(f32[4,128,128]{2,1,0:T(8,128)S(1)} %convolution_subtract_fusion, f32[4,128,256]{2,1,0:T(8,128)} %collective-permute-done), kind=kOutput, calls=%fused_computation.218 | convolution fusion | flops 201326592 | bytes 1310720 | tf_op jit(solution)/shard_map/bij,bjv->biv/dot_general | solution.py:17
  48.6 3.0 %collective-permute-start.1 = (f32[4,128,256]{1,2,0:T(8,128)S(1)}, f32[4,128,256]{1,2,0:T(8,128)S(1)}, u32[]{:S(2)}, u32[]{:S(2)}) collective-permute-start(f32[4,128,256]{1,2,0:T(8,128)S(1)} %pad_maximum_fusion.1), channel_id=1, source_target_pairs={{0,2},{1,3},{2,4},{3,5},{4,6},{5,7},{6,8},{7,9},{8,10},{9,11},{10,... | collective-permute-start | bytes 1572872 | tf_op jit(solution)/shard_map/ppermute | solution.py:13
  52.7 13.0 %collective-permute-done.1 = f32[4,128,256]{1,2,0:T(8,128)S(1)} collective-permute-done((f32[4,128,256]{1,2,0:T(8,128)S(1)}, f32[4,128,256]{1,2,0:T(8,128)S(1)}, u32[]{:S(2)}, u32[]{:S(2)}) %collective-permute-start.1) | collective-permute-done | bytes 524320 | tf_op jit(solution)/shard_map/ppermute | solution.py:13
  66.3 0.8 pad_maximum_fusion.2
  67.1 1.3 collective-permute-start.2
  69.7 11.5 %collective-permute-done.2 = f32[4,128,256]{1,2,0:T(8,128)} collective-permute-done((f32[4,128,256]{1,2,0:T(8,128)}, f32[4,128,256]{1,2,0:T(8,128)}, u32[]{:S(2)}, u32[]{:S(2)}) %collective-permute-start.2) | collective-permute-done | bytes 524320 | tf_op jit(solution)/shard_map/ppermute | solution.py:13
  81.2 1.7 %fusion.75 = f32[4,128,256]{2,1,0:T(8,128)S(1)} fusion(f32[4,128,256]{1,2,0:T(8,128)} %collective-permute-done.2, f32[4,128,256]{1,2,0:T(8,128)S(1)} %fusion.77), kind=kOutput, calls=%fused_computation.198 | convolution fusion | flops 201326592 | bytes 1310720 | tf_op jit(solution)/shard_map/bij,bjv->biv/dot_general | solution.py:17
  83.1 1.3 collective-permute-start.3
  85.3 7.6 %collective-permute-done.3 = f32[4,128,128]{1,2,0:T(8,128)S(1)} collective-permute-done((f32[4,128,128]{1,2,0:T(8,128)S(1)}, f32[4,128,128]{1,2,0:T(8,128)S(1)}, u32[]{:S(2)}, u32[]{:S(2)}) %collective-permute-start.3) | collective-permute-done | bytes 262176 | tf_op jit(solution)/shard_map/ppermute | solution.py:13
  93.6 2.1 %collective-permute-start.4 = (f32[4,128,128]{1,2,0:T(8,128)S(1)}, f32[4,128,128]{1,2,0:T(8,128)S(1)}, u32[]{:S(2)}, u32[]{:S(2)}) collective-permute-start(f32[4,128,128]{1,2,0:T(8,128)S(1)} %convolution_add_fusion.7), channel_id=1, source_target_pairs={{0,1},{1,2},{2,3},{3,4},{4,5},{5,6},{6,7},{7,8},{8,9},{9,10},{10,1... | collective-permute-start | bytes 786440 | tf_op jit(solution)/shard_map/ppermute | solution.py:13
  96.1 8.0 %collective-permute-done.4 = f32[4,128,128]{1,2,0:T(8,128)S(1)} collective-permute-done((f32[4,128,128]{1,2,0:T(8,128)S(1)}, f32[4,128,128]{1,2,0:T(8,128)S(1)}, u32[]{:S(2)}, u32[]{:S(2)}) %collective-permute-start.4) | collective-permute-done | bytes 262176 | tf_op jit(solution)/shard_map/ppermute | solution.py:13
  105.1 0.7 convert_element_type.88
  105.8 15.7 %all-to-all-start = ((bf16[1,32,4,512]{3,2,0,1:T(4,128)(2,1)}), bf16[1,32,4,512]{3,2,0,1:T(4,128)(2,1)S(1)}, u32[]{:S(2)}, u32[]{:S(2)}) async-start(bf16[1,32,4,512]{3,2,0,1:T(4,128)(2,1)} %bitcast.66), calls=%async_computation | async-start | bytes 262144 | tf_op jit(solution)/shard_map/all_to_all | solution.py:184
  122.5 16.0 %all-to-all-done = bf16[1,32,4,512]{3,2,0,1:T(4,128)(2,1)S(1)} async-done(((bf16[1,32,4,512]{3,2,0,1:T(4,128)(2,1)}), bf16[1,32,4,512]{3,2,0,1:T(4,128)(2,1)S(1)}, u32[]{:S(2)}, u32[]{:S(2)}) %all-to-all-start) | async-done | bytes 131104 | tf_op jit(solution)/shard_map/all_to_all | solution.py:184
  140.5 20.2 %all_to_all.14 = bf16[32,1,1,4,512]{4,3,2,1,0:T(4,128)(2,1)S(1)} all-to-all(bf16[32,1,1,4,512]{4,3,2,1,0:T(4,128)(2,1)S(1)} %constant_dynamic-update-slice_fusion), channel_id=1, replica_groups=mesh['line'=32,'scan'=16] {'line'}, dimensions={0} | all-to-all | bytes 262144 | tf_op jit(solution)/shard_map/all_to_all | solution.py:198
  160.6 0.7 reshape_reshape.3
  (227 shorter events, 22.0 us)
Async XLA Ops:
  1.0 25.8 %copy-start.20 = (f32[4,128]{1,0:T(4,128)}, f32[4,128]{1,0:T(4,128)S(1)}, u32[]{:S(2)}) copy-start(f32[4,128]{1,0:T(4,128)S(1)} %sqrt_bitcast_fusion) | copy-start | bytes 6148
  1.1 4.8 %copy-start.17 = (pred[128,128]{1,0:T(8,128)(4,1)}, pred[128,128]{1,0:T(8,128)(4,1)S(1)}, u32[]{:S(2)}) copy-start(pred[128,128]{1,0:T(8,128)(4,1)S(1)} %get-tuple-element.89) | copy-start | bytes 49156
  22.2 2.4 %copy-start.2 = (bf16[1,128,512]{2,1,0:T(8,128)(2,1)S(1)}, bf16[1,128,512]{2,1,0:T(8,128)(2,1)}, u32[]{:S(2)}) copy-start(bf16[1,128,512]{2,1,0:T(8,128)(2,1)} %param.13) | copy-start | bytes 393220
  22.3 2.3 %copy-start.22 = (f32[1,128,4]{1,2,0:T(4,128)S(1)}, f32[1,128,4]{1,2,0:T(4,128)}, u32[]{:S(2)}) copy-start(f32[1,128,4]{1,2,0:T(4,128)} %param.15) | copy-start | bytes 6148
  25.7 6.4 %copy-start.1 = (bf16[1,128,512]{2,1,0:T(8,128)(2,1)S(1)}, bf16[1,128,512]{2,1,0:T(8,128)(2,1)}, u32[]{:S(2)}) copy-start(bf16[1,128,512]{2,1,0:T(8,128)(2,1)} %param.11) | copy-start | bytes 393220
  25.7 7.1 %copy-start.7 = (bf16[32,1,4,512]{3,2,1,0:T(4,128)(2,1)S(1)}, bf16[32,1,4,512]{3,2,1,0:T(4,128)(2,1)}, u32[]{:S(2)}) copy-start(bf16[32,1,4,512]{3,2,1,0:T(4,128)(2,1)} %param.18) | copy-start | bytes 393220
  26.6 6.5 %copy-start.25 = (f32[32,1,4,4]{0,3,2,1:T(4,128)S(1)}, f32[32,1,4,4]{0,3,2,1:T(4,128)}, u32[]{:S(2)}) copy-start(f32[32,1,4,4]{0,3,2,1:T(4,128)} %param.19) | copy-start | bytes 6148
  26.6 6.7 %copy-start.19 = (f32[32,1,4,4]{0,3,2,1:T(4,128)S(1)}, f32[32,1,4,4]{0,3,2,1:T(4,128)}, u32[]{:S(2)}) copy-start(f32[32,1,4,4]{0,3,2,1:T(4,128)} %param.20) | copy-start | bytes 6148
  28.4 18.0 %collective-permute-start = (f32[4,128,256]{2,1,0:T(8,128)}, f32[4,128,256]{2,1,0:T(8,128)}, u32[]{:S(2)}, u32[]{:S(2)}) collective-permute-start(f32[4,128,256]{2,1,0:T(8,128)} %pad_maximum_fusion), channel_id=1, source_target_pairs={{0,1},{1,2},{2,3},{3,4},{4,5},{5,6},{6,7},{7,8},{8,9},{9,10},{10,1... | collective-permute-start | bytes 1572872 | tf_op jit(solution)/shard_map/ppermute | solution.py:13
  48.6 17.1 %collective-permute-start.1 = (f32[4,128,256]{1,2,0:T(8,128)S(1)}, f32[4,128,256]{1,2,0:T(8,128)S(1)}, u32[]{:S(2)}, u32[]{:S(2)}) collective-permute-start(f32[4,128,256]{1,2,0:T(8,128)S(1)} %pad_maximum_fusion.1), channel_id=1, source_target_pairs={{0,2},{1,3},{2,4},{3,5},{4,6},{5,7},{6,8},{7,9},{8,10},{9,11},{10,... | collective-permute-start | bytes 1572872 | tf_op jit(solution)/shard_map/ppermute | solution.py:13
  52.6 15.8 %copy-start.13 = (bf16[1,128,128]{2,1,0:T(8,128)(2,1)S(1)}, bf16[1,128,128]{2,1,0:T(8,128)(2,1)}, u32[]{:S(2)}) copy-start(bf16[1,128,128]{2,1,0:T(8,128)(2,1)} %get-tuple-element.73) | copy-start | bytes 98308
  52.6 15.8 %copy-start.14 = (bf16[1,128,128]{2,1,0:T(8,128)(2,1)S(1)}, bf16[1,128,128]{2,1,0:T(8,128)(2,1)}, u32[]{:S(2)}) copy-start(bf16[1,128,128]{2,1,0:T(8,128)(2,1)} %get-tuple-element.74) | copy-start | bytes 98308
  52.6 15.8 %copy-start.15 = (bf16[1,128,128]{2,1,0:T(8,128)(2,1)S(1)}, bf16[1,128,128]{2,1,0:T(8,128)(2,1)}, u32[]{:S(2)}) copy-start(bf16[1,128,128]{2,1,0:T(8,128)(2,1)} %get-tuple-element.75) | copy-start | bytes 98308
  52.6 15.8 %copy-start.16 = (bf16[1,128,128]{2,1,0:T(8,128)(2,1)S(1)}, bf16[1,128,128]{2,1,0:T(8,128)(2,1)}, u32[]{:S(2)}) copy-start(bf16[1,128,128]{2,1,0:T(8,128)(2,1)} %get-tuple-element.76) | copy-start | bytes 98308
  66.2 2.9 %copy-start.18 = (pred[128,128]{1,0:T(8,128)(4,1)S(1)}, pred[128,128]{1,0:T(8,128)(4,1)}, u32[]{:S(2)}) copy-start(pred[128,128]{1,0:T(8,128)(4,1)} %copy-done.17) | copy-start | bytes 49156
  66.2 2.9 %copy-start.21 = (f32[4,128]{1,0:T(4,128)S(1)}, f32[4,128]{1,0:T(4,128)}, u32[]{:S(2)}) copy-start(f32[4,128]{1,0:T(4,128)} %copy-done.20) | copy-start | bytes 6148
  67.1 14.1 %collective-permute-start.2 = (f32[4,128,256]{1,2,0:T(8,128)}, f32[4,128,256]{1,2,0:T(8,128)}, u32[]{:S(2)}, u32[]{:S(2)}) collective-permute-start(f32[4,128,256]{1,2,0:T(8,128)} %pad_maximum_fusion.2), channel_id=1, source_target_pairs={{0,4},{1,5},{2,6},{3,7},{4,8},{5,9},{6,10},{7,11},{8,12},{9,13},{1... | collective-permute-start | bytes 1572872 | tf_op jit(solution)/shard_map/ppermute | solution.py:13
  82.9 12.8 %copy-start.5 = (f32[1,128,128]{2,1,0:T(8,128)S(1)}, f32[1,128,128]{2,1,0:T(8,128)}, u32[]{:S(2)}) copy-start(f32[1,128,128]{2,1,0:T(8,128)} %get-tuple-element.63) | copy-start | bytes 196612
  82.9 12.8 %copy-start.6 = (f32[1,128,128]{2,1,0:T(8,128)S(1)}, f32[1,128,128]{2,1,0:T(8,128)}, u32[]{:S(2)}) copy-start(f32[1,128,128]{2,1,0:T(8,128)} %get-tuple-element.64) | copy-start | bytes 196612
  83.1 9.8 %collective-permute-start.3 = (f32[4,128,128]{1,2,0:T(8,128)S(1)}, f32[4,128,128]{1,2,0:T(8,128)S(1)}, u32[]{:S(2)}, u32[]{:S(2)}) collective-permute-start(f32[4,128,128]{1,2,0:T(8,128)S(1)} %add.162), channel_id=1, source_target_pairs={{0,8},{1,9},{2,10},{3,11},{4,12},{5,13},{6,14},{7,15},{16,24},{17,... | collective-permute-start | bytes 786440 | tf_op jit(solution)/shard_map/ppermute | solution.py:13
  84.7 20.2 %copy-start.30 = (f32[128]{0:T(128)S(1)}, f32[128]{0:T(128)}, u32[]{:S(2)}) copy-start(f32[128]{0:T(128)} %param.16) | copy-start | bytes 1540
  93.5 28.0 %copy-start.9 = (bf16[4,32,128]{2,1,0:T(8,128)(2,1)S(1)}, bf16[4,32,128]{2,1,0:T(8,128)(2,1)}, u32[]{:S(2)}) copy-start(bf16[4,32,128]{2,1,0:T(8,128)(2,1)} %get-tuple-element.77) | copy-start | bytes 98308
  93.5 28.0 %copy-start.10 = (bf16[4,32,128]{2,1,0:T(8,128)(2,1)S(1)}, bf16[4,32,128]{2,1,0:T(8,128)(2,1)}, u32[]{:S(2)}) copy-start(bf16[4,32,128]{2,1,0:T(8,128)(2,1)} %get-tuple-element.78) | copy-start | bytes 98308
  93.6 28.0 %copy-start.11 = (bf16[4,32,128]{2,1,0:T(8,128)(2,1)S(1)}, bf16[4,32,128]{2,1,0:T(8,128)(2,1)}, u32[]{:S(2)}) copy-start(bf16[4,32,128]{2,1,0:T(8,128)(2,1)} %get-tuple-element.79) | copy-start | bytes 98308
  93.6 28.0 %copy-start.12 = (bf16[4,32,128]{2,1,0:T(8,128)(2,1)S(1)}, bf16[4,32,128]{2,1,0:T(8,128)(2,1)}, u32[]{:S(2)}) copy-start(bf16[4,32,128]{2,1,0:T(8,128)(2,1)} %get-tuple-element.80) | copy-start | bytes 98308
  93.6 28.0 %copy-start.4 = (f32[4,128,128]{2,1,0:T(8,128)S(1)}, f32[4,128,128]{2,1,0:T(8,128)}, u32[]{:S(2)}) copy-start(f32[4,128,128]{2,1,0:T(8,128)} %copy-done.3) | copy-start | bytes 786436
  93.6 28.0 %copy-start.24 = (f32[16,32]{1,0:T(8,128)S(1)}, f32[16,32]{1,0:T(8,128)}, u32[]{:S(2)}) copy-start(f32[16,32]{1,0:T(8,128)} %copy-done.23) | copy-start | bytes 6148
  93.6 28.0 %copy-start.27 = (f32[16,32]{1,0:T(8,128)S(1)}, f32[16,32]{1,0:T(8,128)}, u32[]{:S(2)}) copy-start(f32[16,32]{1,0:T(8,128)} %copy-done.26) | copy-start | bytes 6148
  93.6 28.0 %copy-start.29 = (pred[32,32]{1,0:T(8,128)(4,1)S(1)}, pred[32,32]{1,0:T(8,128)(4,1)}, u32[]{:S(2)}) copy-start(pred[32,32]{1,0:T(8,128)(4,1)} %copy-done.28) | copy-start | bytes 3076
  93.6 10.5 %collective-permute-start.4 = (f32[4,128,128]{1,2,0:T(8,128)S(1)}, f32[4,128,128]{1,2,0:T(8,128)S(1)}, u32[]{:S(2)}, u32[]{:S(2)}) collective-permute-start(f32[4,128,128]{1,2,0:T(8,128)S(1)} %convolution_add_fusion.7), channel_id=1, source_target_pairs={{0,1},{1,2},{2,3},{3,4},{4,5},{5,6},{6,7},{7,8},{8,9},{9,10},{10,1... | collective-permute-start | bytes 786440 | tf_op jit(solution)/shard_map/ppermute | solution.py:13
  105.8 32.8 %all-to-all-start = ((bf16[1,32,4,512]{3,2,0,1:T(4,128)(2,1)}), bf16[1,32,4,512]{3,2,0,1:T(4,128)(2,1)S(1)}, u32[]{:S(2)}, u32[]{:S(2)}) async-start(bf16[1,32,4,512]{3,2,0,1:T(4,128)(2,1)} %bitcast.66), calls=%async_computation | async-start | bytes 262144 | tf_op jit(solution)/shard_map/all_to_all | solution.py:184
  121.6 17.6 %copy-start.31 = (f32[128]{0:T(128)S(1)}, f32[128]{0:T(128)}, u32[]{:S(2)}) copy-start(f32[128]{0:T(128)} %param.21) | copy-start | bytes 1540
  (6 other events, 9.3 us)
